TPU v7x, 32 devices: a whole 2x2x4 slice. The times are simulated.
32 devices in a mesh: dp: 8 (over y, x, core), ctx: 4 (over z).
Axes of the slice: x: 2, y: 2, z: 4, core: 2. Of those that a mesh axis runs over, the one named last changes fastest.
Arguments:
- inputs: bfloat16 [16, 1024, 768], P('dp', 'ctx'), may hold values from -6 to 6
- lengths: int32 [16], P('dp'), may hold values from 921 to 1024, as said below
- ln1_gain: bfloat16 [768], P(('dp', 'ctx')), may hold values from 0.5 to 1.5
- ln1_bias: bfloat16 [768], P(('dp', 'ctx')), may hold values from -4 to 4
- query_weight: bfloat16 [768, 768], P(('dp', 'ctx')), may hold values from -0.3125 to 0.3125
- query_bias: bfloat16 [768], P(('dp', 'ctx')), may hold values from -4 to 4
- key_weight: bfloat16 [768, 768], P(('dp', 'ctx')), may hold values from -0.3125 to 0.3125
- value_weight: bfloat16 [768, 768], P(('dp', 'ctx')), may hold values from -0.21875 to 0.21875
- value_bias: bfloat16 [768], P(('dp', 'ctx')), may hold values from -0.75 to 0.75
- out_weight: bfloat16 [768, 768], P(('dp', 'ctx')), may hold values from -1.75 to 1.75
- out_bias: bfloat16 [768], P(('dp', 'ctx')), may hold values from -4 to 4
- ln2_gain: bfloat16 [768], P(('dp', 'ctx')), may hold values from 0.5 to 1.5
- ln2_bias: bfloat16 [768], P(('dp', 'ctx')), may hold values from -4 to 4
- ffn_in_weight: bfloat16 [768, 3072], P(('dp', 'ctx')), may hold values from -0.21875 to 0.21875
- ffn_in_bias: bfloat16 [3072], P(('dp', 'ctx')), may hold values from -4 to 4
- ffn_out_weight: bfloat16 [3072, 768], P(('dp', 'ctx')), may hold values from -0.15625 to 0.15625
- ffn_out_bias: bfloat16 [768], P(('dp', 'ctx')), may hold values from -4 to 4
- out_grad: bfloat16 [16, 1024, 768], P('dp', 'ctx'), may hold values from -6 to 6
Outputs:
- output: bfloat16 [16, 1024, 768], P('dp', 'ctx')
- input_grad: bfloat16 [16, 1024, 768], P('dp', 'ctx')
- grad_ln1_gain: float32 [768], P(('dp', 'ctx'))
- grad_ln1_bias: float32 [768], P(('dp', 'ctx'))
- grad_query: float32 [768, 768], P(('dp', 'ctx'))
- grad_query_bias: float32 [768], P(('dp', 'ctx'))
- grad_key: float32 [768, 768], P(('dp', 'ctx'))
- grad_value: float32 [768, 768], P(('dp', 'ctx'))
- grad_value_bias: float32 [768], P(('dp', 'ctx'))
- grad_out: float32 [768, 768], P(('dp', 'ctx'))
- grad_out_bias: float32 [768], P(('dp', 'ctx'))
- grad_ln2_gain: float32 [768], P(('dp', 'ctx'))
- grad_ln2_bias: float32 [768], P(('dp', 'ctx'))
- grad_ffn_in: float32 [768, 3072], P(('dp', 'ctx'))
- grad_ffn_in_bias: float32 [3072], P(('dp', 'ctx'))
- grad_ffn_out: float32 [3072, 768], P(('dp', 'ctx'))
- grad_ffn_out_bias: float32 [768], P(('dp', 'ctx'))
Inputs may be any that keep to these rules, and one draw needn't show every extreme that they name: `lengths`: A sequence's molecules occupy positions 0 to its length - 1; some sequence has exactly 1024, some exactly 921.
All inputs are finite; a program needn't handle non-finite values.
Results may differ from a plain program's by a relative error of at most 0.015.
Values may be sent and summed in bfloat16 or wider, within the bound.
No kernel may reach another device: no remote copies, remote signals or barrier semaphores. Data moves between devices by JAX's collectives and lax.ppermute only.
A program may use at most 192 MiB of HBM per device.

v0:
```python
import jax
import jax.numpy as jnp
from jax import lax
from jax.sharding import PartitionSpec as P

H = 12
HD = 64


def layer_norm(tok_rows, gain, shift):
    center = tok_rows - jnp.mean(tok_rows, axis=-1, keepdims=True)
    spread = jnp.mean(center * center, axis=-1, keepdims=True)
    return center * lax.rsqrt(spread + 1e-06) * gain + shift


def gelu_exact(values):
    return jax.nn.gelu(values, approximate=False)


def outer_product(left_rows, right_rows):
    return lax.dot_general(
        left_rows, right_rows, (((0,), (0,)), ((), ())), preferred_element_type=jnp.float32
    )


def back_product(grad_rows, weight):
    return lax.dot_general(
        grad_rows, weight, (((1,), (1,)), ((), ())), preferred_element_type=jnp.float32
    )


def column_sum(grad_rows):
    return jnp.sum(grad_rows.astype(jnp.float32), axis=0)


def fetch(shards):
    return (
        lax.all_gather(shards[0], ("dp", "ctx"), axis=0, tiled=True),
        lax.all_gather(shards[1], ("dp", "ctx"), axis=0, tiled=True),
        lax.all_gather(shards[2], ("dp", "ctx"), axis=0, tiled=True),
        lax.all_gather(shards[3], ("dp", "ctx"), axis=0, tiled=True),
        lax.all_gather(shards[4], ("dp", "ctx"), axis=0, tiled=True),
        lax.all_gather(shards[5], ("dp", "ctx"), axis=0, tiled=True),
        lax.all_gather(shards[6], ("dp", "ctx"), axis=0, tiled=True),
        lax.all_gather(shards[7], ("dp", "ctx"), axis=0, tiled=True),
        lax.all_gather(shards[8], ("dp", "ctx"), axis=0, tiled=True),
        lax.all_gather(shards[9], ("dp", "ctx"), axis=0, tiled=True),
        lax.all_gather(shards[10], ("dp", "ctx"), axis=0, tiled=True),
        lax.all_gather(shards[11], ("dp", "ctx"), axis=0, tiled=True),
        lax.all_gather(shards[12], ("dp", "ctx"), axis=0, tiled=True),
        lax.all_gather(shards[13], ("dp", "ctx"), axis=0, tiled=True),
        lax.all_gather(shards[14], ("dp", "ctx"), axis=0, tiled=True),
    )


def forward(tok_block, length, full_set):
    (
        ln1_gain,
        ln1_bias,
        query_weight,
        query_bias,
        key_weight,
        value_weight,
        value_bias,
        out_weight,
        out_bias,
        ln2_gain,
        ln2_bias,
        ffn_in_weight,
        ffn_in_bias,
        ffn_out_weight,
        ffn_out_bias,
    ) = full_set
    seq_rows = tok_block.shape[0]
    tok_rows = tok_block.astype(jnp.float32)
    normed = layer_norm(
        tok_rows, ln1_gain.astype(jnp.float32), ln1_bias.astype(jnp.float32)
    ).astype(jnp.bfloat16)
    queries = (
        jnp.dot(normed, query_weight, preferred_element_type=jnp.float32)
        + query_bias.astype(jnp.float32)
    ).astype(jnp.bfloat16)
    key_rows = jnp.dot(normed, key_weight, preferred_element_type=jnp.float32).astype(jnp.bfloat16)
    value_rows = (
        jnp.dot(normed, value_weight, preferred_element_type=jnp.float32)
        + value_bias.astype(jnp.float32)
    ).astype(jnp.bfloat16)
    all_keys, all_values = (
        lax.all_gather(key_rows, "ctx", axis=0, tiled=True),
        lax.all_gather(value_rows, "ctx", axis=0, tiled=True),
    )
    total_rows = all_keys.shape[0]
    query_heads = queries.reshape(seq_rows, H, HD)
    key_heads = all_keys.reshape(total_rows, H, HD)
    value_heads = all_values.reshape(total_rows, H, HD)
    scores = jnp.einsum(
        "qhd,khd->hqk", query_heads, key_heads, preferred_element_type=jnp.float32
    ) * HD ** (-0.5)
    valid = jnp.arange(total_rows) < length
    scores = jnp.where(valid[None, None, :], scores, -1e30)
    log_total = jax.nn.logsumexp(scores, axis=-1)
    attn_probs = jax.nn.softmax(scores, axis=-1)
    low_probs = attn_probs.astype(jnp.bfloat16)
    mixed_rows = jnp.einsum(
        "hqk,khd->qhd", low_probs, value_heads, preferred_element_type=jnp.float32
    )
    mixed_rows = mixed_rows.reshape(seq_rows, H * HD).astype(jnp.bfloat16)
    middle = (
        tok_rows
        + jnp.dot(mixed_rows, out_weight, preferred_element_type=jnp.float32)
        + out_bias.astype(jnp.float32)
    )
    normed_two = layer_norm(
        middle, ln2_gain.astype(jnp.float32), ln2_bias.astype(jnp.float32)
    ).astype(jnp.bfloat16)
    ffn_pre = jnp.dot(
        normed_two, ffn_in_weight, preferred_element_type=jnp.float32
    ) + ffn_in_bias.astype(jnp.float32)
    ffn_act = gelu_exact(ffn_pre).astype(jnp.bfloat16)
    result = (
        middle
        + jnp.dot(ffn_act, ffn_out_weight, preferred_element_type=jnp.float32)
        + ffn_out_bias.astype(jnp.float32)
    )
    kept = (
        tok_rows,
        normed,
        query_heads,
        key_heads,
        value_heads,
        attn_probs,
        low_probs,
        mixed_rows,
        middle,
        normed_two,
        ffn_pre,
        ffn_act,
        log_total,
        length,
    )
    return (result.astype(jnp.bfloat16), kept)


def backward(kept, cot_block, full_set):
    (
        ln1_gain,
        ln1_bias,
        query_weight,
        query_bias,
        key_weight,
        value_weight,
        value_bias,
        out_weight,
        out_bias,
        ln2_gain,
        ln2_bias,
        ffn_in_weight,
        ffn_in_bias,
        ffn_out_weight,
        ffn_out_bias,
    ) = full_set
    (
        tok_rows,
        normed,
        query_heads,
        key_heads,
        value_heads,
        attn_probs,
        low_probs,
        mixed_rows,
        middle,
        normed_two,
        ffn_pre,
        ffn_act,
        log_total,
        length,
    ) = kept
    seq_rows = tok_rows.shape[0]
    total_rows = key_heads.shape[0]
    score_scale = HD ** (-0.5)
    d_out = cot_block.astype(jnp.float32)
    d_ffn_out = d_out.astype(jnp.bfloat16)
    grad_ffn_out_bias = column_sum(d_ffn_out)
    grad_ffn_out = outer_product(ffn_act, d_ffn_out)
    d_act = back_product(d_ffn_out, ffn_out_weight)
    unused, gelu_back = jax.vjp(gelu_exact, ffn_pre)
    d_pre = gelu_back(d_act)[0].astype(jnp.bfloat16)
    grad_ffn_in_bias = column_sum(d_pre)
    grad_ffn_in = outer_product(normed_two, d_pre)
    d_normed_two = back_product(d_pre, ffn_in_weight)
    unused, second_back = jax.vjp(
        layer_norm, middle, ln2_gain.astype(jnp.float32), ln2_bias.astype(jnp.float32)
    )
    d_middle, grad_ln2_gain, grad_ln2_bias = second_back(d_normed_two)
    d_middle = d_middle + d_out
    d_branch = d_middle.astype(jnp.bfloat16)
    grad_out_bias = column_sum(d_branch)
    grad_out = outer_product(mixed_rows, d_branch)
    d_mixed = back_product(d_branch, out_weight).astype(jnp.bfloat16).reshape(seq_rows, H, HD)
    d_probs = jnp.einsum("qhd,khd->hqk", d_mixed, value_heads, preferred_element_type=jnp.float32)
    row_inner = jnp.sum(attn_probs * d_probs, axis=-1, keepdims=True)
    d_scores = (attn_probs * (d_probs - row_inner)).astype(jnp.bfloat16)
    d_query = (
        jnp.einsum("hqk,khd->qhd", d_scores, key_heads, preferred_element_type=jnp.float32)
        * score_scale
    )
    d_query = d_query.reshape(seq_rows, H * HD).astype(jnp.bfloat16)
    key_terms = (
        jnp.einsum("hqk,qhd->khd", d_scores, query_heads, preferred_element_type=jnp.float32)
        * score_scale
    )
    value_terms = jnp.einsum("hqk,qhd->khd", low_probs, d_mixed, preferred_element_type=jnp.float32)
    key_sums, value_sums = (
        lax.psum_scatter(
            key_terms.reshape(total_rows, H * HD).astype(jnp.bfloat16),
            "ctx",
            scatter_dimension=0,
            tiled=True,
        ).astype(jnp.float32),
        lax.psum_scatter(
            value_terms.reshape(total_rows, H * HD).astype(jnp.bfloat16),
            "ctx",
            scatter_dimension=0,
            tiled=True,
        ).astype(jnp.float32),
    )
    d_key = key_sums.astype(jnp.bfloat16)
    d_value = value_sums.astype(jnp.bfloat16)
    grad_query_bias = column_sum(d_query)
    grad_value_bias = column_sum(d_value)
    grad_query = outer_product(normed, d_query)
    grad_key = outer_product(normed, d_key)
    grad_value = outer_product(normed, d_value)
    d_normed = (
        back_product(d_query, query_weight)
        + back_product(d_key, key_weight)
        + back_product(d_value, value_weight)
    )
    unused, first_back = jax.vjp(
        layer_norm, tok_rows, ln1_gain.astype(jnp.float32), ln1_bias.astype(jnp.float32)
    )
    d_rows, grad_ln1_gain, grad_ln1_bias = first_back(d_normed)
    d_input = (d_middle + d_rows).astype(jnp.bfloat16)
    grads = (
        grad_ln1_gain,
        grad_ln1_bias,
        grad_query,
        grad_query_bias,
        grad_key,
        grad_value,
        grad_value_bias,
        grad_out,
        grad_out_bias,
        grad_ln2_gain,
        grad_ln2_bias,
        grad_ffn_in,
        grad_ffn_in_bias,
        grad_ffn_out,
        grad_ffn_out_bias,
    )
    return (d_input, grads)


def per_device(
    inputs,
    lengths,
    ln1_gain,
    ln1_bias,
    query_weight,
    query_bias,
    key_weight,
    value_weight,
    value_bias,
    out_weight,
    out_bias,
    ln2_gain,
    ln2_bias,
    ffn_in_weight,
    ffn_in_bias,
    ffn_out_weight,
    ffn_out_bias,
    out_grad,
):
    shards = (
        ln1_gain,
        ln1_bias,
        query_weight,
        query_bias,
        key_weight,
        value_weight,
        value_bias,
        out_weight,
        out_bias,
        ln2_gain,
        ln2_bias,
        ffn_in_weight,
        ffn_in_bias,
        ffn_out_weight,
        ffn_out_bias,
    )

    def forward_step(counter, seq_entry):
        tok_block, length = seq_entry
        result, kept = forward(tok_block, length, fetch(shards))
        return (counter, result)

    counter, output = lax.scan(forward_step, jnp.zeros((), jnp.int32), (inputs, lengths))

    def backward_step(totals, seq_entry):
        tok_block, length, cot_block = seq_entry
        full_set = fetch(shards)
        unused, kept = forward(tok_block, length, full_set)
        d_input, grads = backward(kept, cot_block, full_set)
        return (jax.tree.map(jnp.add, totals, grads), d_input)

    groups = lax.axis_size(("dp", "ctx"))
    start_totals = tuple(
        (
            jnp.zeros((shard_item.shape[0] * groups,) + shard_item.shape[1:], jnp.float32)
            for shard_item in shards
        )
    )
    totals, input_grad = lax.scan(backward_step, start_totals, (inputs, lengths, out_grad))
    grad_shards = lax.psum_scatter(totals, ("dp", "ctx"), scatter_dimension=0, tiled=True)
    return (output, input_grad) + tuple(grad_shards)


def solution(mesh):
    return jax.shard_map(
        per_device,
        mesh=mesh,
        in_specs=(
            P("dp", "ctx", None),
            P("dp"),
            P(("dp", "ctx")),
            P(("dp", "ctx")),
            P(("dp", "ctx"), None),
            P(("dp", "ctx")),
            P(("dp", "ctx"), None),
            P(("dp", "ctx"), None),
            P(("dp", "ctx")),
            P(("dp", "ctx"), None),
            P(("dp", "ctx")),
            P(("dp", "ctx")),
            P(("dp", "ctx")),
            P(("dp", "ctx"), None),
            P(("dp", "ctx")),
            P(("dp", "ctx"), None),
            P(("dp", "ctx")),
            P("dp", "ctx", None),
        ),
        out_specs=(
            P("dp", "ctx", None),
            P("dp", "ctx", None),
            P(("dp", "ctx")),
            P(("dp", "ctx")),
            P(("dp", "ctx"), None),
            P(("dp", "ctx")),
            P(("dp", "ctx"), None),
            P(("dp", "ctx"), None),
            P(("dp", "ctx")),
            P(("dp", "ctx"), None),
            P(("dp", "ctx")),
            P(("dp", "ctx")),
            P(("dp", "ctx")),
            P(("dp", "ctx"), None),
            P(("dp", "ctx")),
            P(("dp", "ctx"), None),
            P(("dp", "ctx")),
        ),
        check_vma=False,
    )
```

profile of v0, /device:TPU:0, one launch (start us, length us, event | category | flops | bytes accessed | tf_op | source)
XLA Modules:
  0.0 2723.2 jit_solution(3749500177245971645)
XLA Ops:
  8.2 888.4 %while.51 = (s32[]{:T(128)}, bf16[2,256,768]{2,1,0:T(8,128)(2,1)S(1)}, bf16[2,256,768]{2,1,0:T(8,128)(2,1)}, bf16[24]{0:T(256)(128)(2,1)}, bf16[24]{0:T(256)(128...) while((s32[]{:T(128)}, ...), condition=%wide.region_7.8_spmd, body=%wide.region_0.7_spmd.sunk | while | flops 4508832256 | bytes 116793320 | solution.py:307
  18.1 42.5 %all-reduce.39 = (bf16[768]{0:T(1024)(128)(2,1)S(1)}, bf16[768]{0:T(1024)(128)(2,1)S(1)}, bf16[768]{0:T(1024)(128)(2,1)S(1)}, bf16[768]{0:T(1024)(128)(2,1)S(1)}...) all-reduce(bf16[768]{0:T(1024)(128)(2,1)S(1)} %dynamic-update-slice, ...), channel_id=1, replica_groups=mesh['dp'=8,'ctx'=4] {'dp','ctx'}, use_global_device_ids=true, to_apply=%add.2 | all-reduce | flops 9216 | bytes 36864 | tf_op jit(solution)/shard_map/while
  71.7 52.9 %all-gather.17.cloned.1.call-done = bf16[768,768]{1,0:T(8,128)(2,1)} async-done(((bf16[24,768]{1,0:T(8,128)(2,1)}), bf16[768,768]{1,0:T(8,128)(2,1)}) %all-gather.17.cloned.1.call-update) | async-done | bytes 1179664 | tf_op jit(solution)/shard_map/while/body/eval_jaxpr/all_gather | solution.py:43
  132.9 47.5 %all-gather.21.cloned.1.call-done = bf16[768,768]{1,0:T(8,128)(2,1)} async-done(((bf16[24,768]{1,0:T(8,128)(2,1)}), bf16[768,768]{1,0:T(8,128)(2,1)}) %all-gather.21.cloned.1.call-update) | async-done | bytes 1179664 | tf_op jit(solution)/shard_map/while/body/eval_jaxpr/all_gather | solution.py:40
  182.3 36.0 %all-gather.25.cloned.1.call-done = bf16[1024,768]{1,0:T(8,128)(2,1)} async-done(((bf16[256,768]{1,0:T(8,128)(2,1)}), bf16[1024,768]{1,0:T(8,128)(2,1)}) %all-gather.25.cloned.1.call-update) | async-done | bytes 1572880 | tf_op jit(solution)/shard_map/while/body/eval_jaxpr/all_gather | solution.py:89
  220.0 36.2 %all-gather.19.cloned.1.call-done = bf16[1024,768]{1,0:T(8,128)(2,1)} async-done(((bf16[256,768]{1,0:T(8,128)(2,1)}), bf16[1024,768]{1,0:T(8,128)(2,1)}) %all-gather.19.cloned.1.call-update) | async-done | bytes 1572880 | tf_op jit(solution)/shard_map/while/body/eval_jaxpr/all_gather | solution.py:90
  274.2 37.6 %all-gather.27.cloned.1.call-done = bf16[768,768]{1,0:T(8,128)(2,1)} async-done(((bf16[24,768]{1,0:T(8,128)(2,1)}), bf16[768,768]{1,0:T(8,128)(2,1)}) %all-gather.27.cloned.1.call-update) | async-done | bytes 1179664 | tf_op jit(solution)/shard_map/while/body/eval_jaxpr/all_gather | solution.py:45
  313.9 63.2 %all-gather.29.cloned.1.call-done = bf16[3072,768]{1,0:T(8,128)(2,1)} async-done(((bf16[96,768]{1,0:T(8,128)(2,1)}), bf16[3072,768]{1,0:T(8,128)(2,1)}) %all-gather.29.cloned.1.call-update) | async-done | bytes 4718608 | tf_op jit(solution)/shard_map/while/body/eval_jaxpr/all_gather | solution.py:51
  377.1 64.7 %all-gather.31.cloned.1.call-done = bf16[768,3072]{1,0:T(8,128)(2,1)} async-done(((bf16[24,3072]{1,0:T(8,128)(2,1)}), bf16[768,3072]{1,0:T(8,128)(2,1)}) %all-gather.31.cloned.1.call-update) | async-done | bytes 4718608 | tf_op jit(solution)/shard_map/while/body/eval_jaxpr/all_gather | solution.py:49
  441.9 12.9 fusion.316
  464.4 39.8 %all-reduce.39 = (bf16[768]{0:T(1024)(128)(2,1)S(1)}, bf16[768]{0:T(1024)(128)(2,1)S(1)}, bf16[768]{0:T(1024)(128)(2,1)S(1)}, bf16[768]{0:T(1024)(128)(2,1)S(1)}...) all-reduce(bf16[768]{0:T(1024)(128)(2,1)S(1)} %dynamic-update-slice, ...), channel_id=1, replica_groups=mesh['dp'=8,'ctx'=4] {'dp','ctx'}, use_global_device_ids=true, to_apply=%add.2 | all-reduce | flops 9216 | bytes 36864 | tf_op jit(solution)/shard_map/while
  513.7 52.9 %all-gather.17.cloned.1.call-done = bf16[768,768]{1,0:T(8,128)(2,1)} async-done(((bf16[24,768]{1,0:T(8,128)(2,1)}), bf16[768,768]{1,0:T(8,128)(2,1)}) %all-gather.17.cloned.1.call-update) | async-done | bytes 1179664 | tf_op jit(solution)/shard_map/while/body/eval_jaxpr/all_gather | solution.py:43
  574.6 47.8 %all-gather.21.cloned.1.call-done = bf16[768,768]{1,0:T(8,128)(2,1)} async-done(((bf16[24,768]{1,0:T(8,128)(2,1)}), bf16[768,768]{1,0:T(8,128)(2,1)}) %all-gather.21.cloned.1.call-update) | async-done | bytes 1179664 | tf_op jit(solution)/shard_map/while/body/eval_jaxpr/all_gather | solution.py:40
  624.4 36.0 %all-gather.25.cloned.1.call-done = bf16[1024,768]{1,0:T(8,128)(2,1)} async-done(((bf16[256,768]{1,0:T(8,128)(2,1)}), bf16[1024,768]{1,0:T(8,128)(2,1)}) %all-gather.25.cloned.1.call-update) | async-done | bytes 1572880 | tf_op jit(solution)/shard_map/while/body/eval_jaxpr/all_gather | solution.py:89
  662.1 36.3 %all-gather.19.cloned.1.call-done = bf16[1024,768]{1,0:T(8,128)(2,1)} async-done(((bf16[256,768]{1,0:T(8,128)(2,1)}), bf16[1024,768]{1,0:T(8,128)(2,1)}) %all-gather.19.cloned.1.call-update) | async-done | bytes 1572880 | tf_op jit(solution)/shard_map/while/body/eval_jaxpr/all_gather | solution.py:90
  716.4 37.6 %all-gather.27.cloned.1.call-done = bf16[768,768]{1,0:T(8,128)(2,1)} async-done(((bf16[24,768]{1,0:T(8,128)(2,1)}), bf16[768,768]{1,0:T(8,128)(2,1)}) %all-gather.27.cloned.1.call-update) | async-done | bytes 1179664 | tf_op jit(solution)/shard_map/while/body/eval_jaxpr/all_gather | solution.py:45
  756.1 63.1 %all-gather.29.cloned.1.call-done = bf16[3072,768]{1,0:T(8,128)(2,1)} async-done(((bf16[96,768]{1,0:T(8,128)(2,1)}), bf16[3072,768]{1,0:T(8,128)(2,1)}) %all-gather.29.cloned.1.call-update) | async-done | bytes 4718608 | tf_op jit(solution)/shard_map/while/body/eval_jaxpr/all_gather | solution.py:51
  819.2 64.6 %all-gather.31.cloned.1.call-done = bf16[768,3072]{1,0:T(8,128)(2,1)} async-done(((bf16[24,3072]{1,0:T(8,128)(2,1)}), bf16[768,3072]{1,0:T(8,128)(2,1)}) %all-gather.31.cloned.1.call-update) | async-done | bytes 4718608 | tf_op jit(solution)/shard_map/while/body/eval_jaxpr/all_gather | solution.py:49
  883.8 12.9 fusion.316
  897.8 1116.4 %while.52 = (s32[]{:T(128)}, f32[768]{0:T(1024)}, f32[768]{0:T(1024)}, f32[768,768]{1,0:T(8,128)}, f32[768]{0:T(1024)}, /*index=5*/f32[768,768]{1,0:T(8,128)}, f...) while((s32[]{:T(128)}, f32[768]{0:T(1024)}, ...), condition=%wide.region_31.32_spmd.clone, body=%wide.region_8.31_spmd.clone.sunk | while | flops 12278196224 | bytes 516163296 | solution.py:323
  930.1 39.5 %all-reduce.40 = (bf16[768]{0:T(1024)(128)(2,1)S(1)}, bf16[768]{0:T(1024)(128)(2,1)S(1)}, bf16[3072]{0:T(1024)(128)(2,1)S(1)}, bf16[768]{0:T(1024)(128)(2,1)S(1)...) all-reduce(bf16[768]{0:T(1024)(128)(2,1)S(1)} %dynamic-update-slice, ...), channel_id=1, replica_groups=mesh['dp'=8,'ctx'=4] {'dp','ctx'}, use_global_device_ids=true, to_apply=%add.10 | all-reduce | flops 8448 | bytes 33792 | tf_op jit(solution)/shard_map/while
  980.1 52.9 %all-gather.33.cloned.1.call-done = bf16[768,768]{1,0:T(8,128)(2,1)} async-done(((bf16[24,768]{1,0:T(8,128)(2,1)}), bf16[768,768]{1,0:T(8,128)(2,1)}) %all-gather.33.cloned.1.call-update) | async-done | bytes 1179664 | tf_op jit(solution)/shard_map/while/body/eval_jaxpr/all_gather | solution.py:42
  1039.0 49.7 %all-gather.37.cloned.1.call-done = bf16[768,768]{1,0:T(8,128)(2,1)} async-done(((bf16[24,768]{1,0:T(8,128)(2,1)}), bf16[768,768]{1,0:T(8,128)(2,1)}) %all-gather.37.cloned.1.call-update) | async-done | bytes 1179664 | tf_op jit(solution)/shard_map/while/body/eval_jaxpr/all_gather | solution.py:40
  1090.7 35.4 %all-gather.41.cloned.1.call-done = bf16[1024,768]{1,0:T(8,128)(2,1)} async-done(((bf16[256,768]{1,0:T(8,128)(2,1)}), bf16[1024,768]{1,0:T(8,128)(2,1)}) %all-gather.41.cloned.1.call-update) | async-done | bytes 1572880 | tf_op jit(solution)/shard_map/while/body/eval_jaxpr/all_gather | solution.py:90
  1128.7 34.9 %all-gather.35.cloned.1.call-done = bf16[1024,768]{1,0:T(8,128)(2,1)} async-done(((bf16[256,768]{1,0:T(8,128)(2,1)}), bf16[1024,768]{1,0:T(8,128)(2,1)}) %all-gather.35.cloned.1.call-update) | async-done | bytes 1572880 | tf_op jit(solution)/shard_map/while/body/eval_jaxpr/all_gather | solution.py:89
  1179.5 39.8 %all-gather.43.cloned.1.call-done = bf16[768,768]{1,0:T(8,128)(2,1)} async-done(((bf16[24,768]{1,0:T(8,128)(2,1)}), bf16[768,768]{1,0:T(8,128)(2,1)}) %all-gather.43.cloned.1.call-update) | async-done | bytes 1179664 | tf_op jit(solution)/shard_map/while/body/eval_jaxpr/all_gather | solution.py:45
  1221.4 63.2 %all-gather.45.cloned.1.call-done = bf16[768,3072]{1,0:T(8,128)(2,1)} async-done(((bf16[24,3072]{1,0:T(8,128)(2,1)}), bf16[768,3072]{1,0:T(8,128)(2,1)}) %all-gather.45.cloned.1.call-update) | async-done | bytes 4718608 | tf_op jit(solution)/shard_map/while/body/eval_jaxpr/all_gather | solution.py:49
  1290.1 59.1 %all-gather.47.cloned.1.call-done = bf16[3072,768]{1,0:T(8,128)(2,1)} async-done(((bf16[96,768]{1,0:T(8,128)(2,1)}), bf16[3072,768]{1,0:T(8,128)(2,1)}) %all-gather.47.cloned.1.call-update) | async-done | bytes 4718608 | tf_op jit(solution)/shard_map/while/body/eval_jaxpr/all_gather | solution.py:51
  1349.2 11.1 convert_reduce_fusion.15
  1431.0 28.6 %reduce-scatter.23.cloned.1.call-done = bf16[256,768]{0,1:T(8,128)(2,1)} async-done(((bf16[1024,768]{0,1:T(8,128)(2,1)}), bf16[256,768]{0,1:T(8,128)(2,1)}) %reduce-scatter.23.cloned.1.call-update) | async-done | bytes 393232 | tf_op jit(solution)/shard_map/while/body/eval_jaxpr/reduce_scatter | solution.py:220
  1476.3 39.7 %all-reduce.40 = (bf16[768]{0:T(1024)(128)(2,1)S(1)}, bf16[768]{0:T(1024)(128)(2,1)S(1)}, bf16[3072]{0:T(1024)(128)(2,1)S(1)}, bf16[768]{0:T(1024)(128)(2,1)S(1)...) all-reduce(bf16[768]{0:T(1024)(128)(2,1)S(1)} %dynamic-update-slice, ...), channel_id=1, replica_groups=mesh['dp'=8,'ctx'=4] {'dp','ctx'}, use_global_device_ids=true, to_apply=%add.10 | all-reduce | flops 8448 | bytes 33792 | tf_op jit(solution)/shard_map/while
  1526.7 53.0 %all-gather.33.cloned.1.call-done = bf16[768,768]{1,0:T(8,128)(2,1)} async-done(((bf16[24,768]{1,0:T(8,128)(2,1)}), bf16[768,768]{1,0:T(8,128)(2,1)}) %all-gather.33.cloned.1.call-update) | async-done | bytes 1179664 | tf_op jit(solution)/shard_map/while/body/eval_jaxpr/all_gather | solution.py:42
  1585.7 49.7 %all-gather.37.cloned.1.call-done = bf16[768,768]{1,0:T(8,128)(2,1)} async-done(((bf16[24,768]{1,0:T(8,128)(2,1)}), bf16[768,768]{1,0:T(8,128)(2,1)}) %all-gather.37.cloned.1.call-update) | async-done | bytes 1179664 | tf_op jit(solution)/shard_map/while/body/eval_jaxpr/all_gather | solution.py:40
  1637.4 35.4 %all-gather.41.cloned.1.call-done = bf16[1024,768]{1,0:T(8,128)(2,1)} async-done(((bf16[256,768]{1,0:T(8,128)(2,1)}), bf16[1024,768]{1,0:T(8,128)(2,1)}) %all-gather.41.cloned.1.call-update) | async-done | bytes 1572880 | tf_op jit(solution)/shard_map/while/body/eval_jaxpr/all_gather | solution.py:90
  1675.4 34.9 %all-gather.35.cloned.1.call-done = bf16[1024,768]{1,0:T(8,128)(2,1)} async-done(((bf16[256,768]{1,0:T(8,128)(2,1)}), bf16[1024,768]{1,0:T(8,128)(2,1)}) %all-gather.35.cloned.1.call-update) | async-done | bytes 1572880 | tf_op jit(solution)/shard_map/while/body/eval_jaxpr/all_gather | solution.py:89
  1726.2 39.8 %all-gather.43.cloned.1.call-done = bf16[768,768]{1,0:T(8,128)(2,1)} async-done(((bf16[24,768]{1,0:T(8,128)(2,1)}), bf16[768,768]{1,0:T(8,128)(2,1)}) %all-gather.43.cloned.1.call-update) | async-done | bytes 1179664 | tf_op jit(solution)/shard_map/while/body/eval_jaxpr/all_gather | solution.py:45
  1768.1 63.1 %all-gather.45.cloned.1.call-done = bf16[768,3072]{1,0:T(8,128)(2,1)} async-done(((bf16[24,3072]{1,0:T(8,128)(2,1)}), bf16[768,3072]{1,0:T(8,128)(2,1)}) %all-gather.45.cloned.1.call-update) | async-done | bytes 4718608 | tf_op jit(solution)/shard_map/while/body/eval_jaxpr/all_gather | solution.py:49
  1836.7 59.3 %all-gather.47.cloned.1.call-done = bf16[3072,768]{1,0:T(8,128)(2,1)} async-done(((bf16[96,768]{1,0:T(8,128)(2,1)}), bf16[3072,768]{1,0:T(8,128)(2,1)}) %all-gather.47.cloned.1.call-update) | async-done | bytes 4718608 | tf_op jit(solution)/shard_map/while/body/eval_jaxpr/all_gather | solution.py:51
  1895.9 11.1 convert_reduce_fusion.15
  1970.9 12.1 select_add_fusion.38
  1985.0 21.3 reduce-scatter.23.cloned.1.call-done
  2018.2 40.0 %all-reduce.36 = (f32[768]{0:T(1024)S(1)}, f32[768]{0:T(1024)S(1)}, f32[768]{0:T(1024)S(1)}, f32[768]{0:T(1024)S(1)}, f32[768]{0:T(1024)S(1)}, /*index=5*/f32[76...) all-reduce(f32[768]{0:T(1024)S(1)} %copy-done.57, ...), channel_id=4, replica_groups=mesh['dp'=8,'ctx'=4] {'dp','ctx'}, use_global_device_ids=true, to_apply=%region_32.33.clone | all-reduce | flops 9216 | bytes 73728
  2063.5 55.5 %reduce-scatter.9.cloned.1.call-done = f32[24,768]{1,0:T(8,128)} async-done(((f32[768,768]{1,0:T(8,128)}), f32[24,768]{1,0:T(8,128)}) %reduce-scatter.9.cloned.1.call-update) | async-done | bytes 73744 | tf_op jit(solution)/shard_map/reduce_scatter | solution.py:324
  2119.1 104.4 %reduce-scatter.11.cloned.1.call-done = f32[24,768]{1,0:T(8,128)} async-done(((f32[768,768]{1,0:T(8,128)}), f32[24,768]{1,0:T(8,128)}) %reduce-scatter.11.cloned.1.call-update) | async-done | bytes 73744 | tf_op jit(solution)/shard_map/reduce_scatter | solution.py:324
  2223.5 104.3 %reduce-scatter.13.cloned.1.call-done = f32[24,768]{1,0:T(8,128)} async-done(((f32[768,768]{1,0:T(8,128)}), f32[24,768]{1,0:T(8,128)}) %reduce-scatter.13.cloned.1.call-update) | async-done | bytes 73744 | tf_op jit(solution)/shard_map/reduce_scatter | solution.py:324
  2327.8 104.5 %reduce-scatter.15.cloned.1.call-done = f32[24,768]{1,0:T(8,128)} async-done(((f32[768,768]{1,0:T(8,128)}), f32[24,768]{1,0:T(8,128)}) %reduce-scatter.15.cloned.1.call-update) | async-done | bytes 73744 | tf_op jit(solution)/shard_map/reduce_scatter | solution.py:324
  2432.3 141.7 %reduce-scatter.17.cloned.1.call-done = f32[24,3072]{1,0:T(8,128)} async-done(((f32[768,3072]{1,0:T(8,128)}), f32[24,3072]{1,0:T(8,128)}) %reduce-scatter.17.cloned.1.call-update) | async-done | bytes 294928 | tf_op jit(solution)/shard_map/reduce_scatter | solution.py:324
  2574.0 141.7 %reduce-scatter.19.cloned.1.call-done = f32[96,768]{1,0:T(8,128)} async-done(((f32[3072,768]{1,0:T(8,128)}), f32[96,768]{1,0:T(8,128)}) %reduce-scatter.19.cloned.1.call-update) | async-done | bytes 294928 | tf_op jit(solution)/shard_map/reduce_scatter | solution.py:324
  (623 shorter events, 371.3 us)
Async XLA Ops:
  8.2 60.6 %all-gather.23.cloned.1.call-start = ((), (), s32[]{:S(2)}) async-start(), calls=%async_computation.17 | async-start | bytes 1216512 | tf_op jit(solution)/shard_map/while/body/eval_jaxpr/all_gather | solution.py:42
  9.0 115.6 %all-gather.17.cloned.1.call-start = ((), (), s32[]{:S(2)}) async-start(), calls=%async_computation.14 | async-start | bytes 1216512 | tf_op jit(solution)/shard_map/while/body/eval_jaxpr/all_gather | solution.py:43
  9.7 170.6 %all-gather.21.cloned.1.call-start = ((), (), s32[]{:S(2)}) async-start(), calls=%async_computation.16 | async-start | bytes 1216512 | tf_op jit(solution)/shard_map/while/body/eval_jaxpr/all_gather | solution.py:40
  10.5 207.8 %all-gather.25.cloned.1.call-start = ((), (), s32[]{:S(2)}) async-start(), calls=%async_computation.18 | async-start | bytes 1966080 | tf_op jit(solution)/shard_map/while/body/eval_jaxpr/all_gather | solution.py:89
  71.6 184.6 %all-gather.19.cloned.1.call-start = ((), (), s32[]{:S(2)}) async-start(), calls=%async_computation.15 | async-start | bytes 1966080 | tf_op jit(solution)/shard_map/while/body/eval_jaxpr/all_gather | solution.py:90
  127.2 184.6 %all-gather.27.cloned.1.call-start = ((), (), s32[]{:S(2)}) async-start(), calls=%async_computation.19 | async-start | bytes 1216512 | tf_op jit(solution)/shard_map/while/body/eval_jaxpr/all_gather | solution.py:45
  127.8 249.4 %all-gather.29.cloned.1.call-start = ((), (), s32[]{:S(2)}) async-start(), calls=%async_computation.20 | async-start | bytes 4866048 | tf_op jit(solution)/shard_map/while/body/eval_jaxpr/all_gather | solution.py:51
  128.5 313.3 %all-gather.31.cloned.1.call-start = ((), (), s32[]{:S(2)}) async-start(), calls=%async_computation.21 | async-start | bytes 4866048 | tf_op jit(solution)/shard_map/while/body/eval_jaxpr/all_gather | solution.py:49
  274.2 167.7 %copy-start.60 = (f32[768]{0:T(1024)S(1)}, f32[768]{0:T(1024)}, u32[]{:S(2)}) copy-start(f32[768]{0:T(1024)} %convert_element_type.492) | copy-start | bytes 9220 | tf_op jit(solution)/shard_map/while
  274.2 167.7 %copy-start.61 = (f32[768]{0:T(1024)S(1)}, f32[768]{0:T(1024)}, u32[]{:S(2)}) copy-start(f32[768]{0:T(1024)} %convert_element_type.493) | copy-start | bytes 9220 | tf_op jit(solution)/shard_map/while
  274.2 167.7 %copy-start.62 = (f32[768]{0:T(1024)S(1)}, f32[768]{0:T(1024)}, u32[]{:S(2)}) copy-start(f32[768]{0:T(1024)} %convert_element_type.494) | copy-start | bytes 9220 | tf_op jit(solution)/shard_map/while
  454.8 56.2 %all-gather.23.cloned.1.call-start = ((), (), s32[]{:S(2)}) async-start(), calls=%async_computation.17 | async-start | bytes 1216512 | tf_op jit(solution)/shard_map/while/body/eval_jaxpr/all_gather | solution.py:42
  455.5 111.1 %all-gather.17.cloned.1.call-start = ((), (), s32[]{:S(2)}) async-start(), calls=%async_computation.14 | async-start | bytes 1216512 | tf_op jit(solution)/shard_map/while/body/eval_jaxpr/all_gather | solution.py:43
  456.1 166.3 %all-gather.21.cloned.1.call-start = ((), (), s32[]{:S(2)}) async-start(), calls=%async_computation.16 | async-start | bytes 1216512 | tf_op jit(solution)/shard_map/while/body/eval_jaxpr/all_gather | solution.py:40
  456.8 203.5 %all-gather.25.cloned.1.call-start = ((), (), s32[]{:S(2)}) async-start(), calls=%async_computation.18 | async-start | bytes 1966080 | tf_op jit(solution)/shard_map/while/body/eval_jaxpr/all_gather | solution.py:89
  513.7 184.7 %all-gather.19.cloned.1.call-start = ((), (), s32[]{:S(2)}) async-start(), calls=%async_computation.15 | async-start | bytes 1966080 | tf_op jit(solution)/shard_map/while/body/eval_jaxpr/all_gather | solution.py:90
  569.2 184.7 %all-gather.27.cloned.1.call-start = ((), (), s32[]{:S(2)}) async-start(), calls=%async_computation.19 | async-start | bytes 1216512 | tf_op jit(solution)/shard_map/while/body/eval_jaxpr/all_gather | solution.py:45
  569.8 249.4 %all-gather.29.cloned.1.call-start = ((), (), s32[]{:S(2)}) async-start(), calls=%async_computation.20 | async-start | bytes 4866048 | tf_op jit(solution)/shard_map/while/body/eval_jaxpr/all_gather | solution.py:51
  570.4 313.4 %all-gather.31.cloned.1.call-start = ((), (), s32[]{:S(2)}) async-start(), calls=%async_computation.21 | async-start | bytes 4866048 | tf_op jit(solution)/shard_map/while/body/eval_jaxpr/all_gather | solution.py:49
  716.4 167.4 %copy-start.60 = (f32[768]{0:T(1024)S(1)}, f32[768]{0:T(1024)}, u32[]{:S(2)}) copy-start(f32[768]{0:T(1024)} %convert_element_type.492) | copy-start | bytes 9220 | tf_op jit(solution)/shard_map/while
  716.4 167.4 %copy-start.61 = (f32[768]{0:T(1024)S(1)}, f32[768]{0:T(1024)}, u32[]{:S(2)}) copy-start(f32[768]{0:T(1024)} %convert_element_type.493) | copy-start | bytes 9220 | tf_op jit(solution)/shard_map/while
  716.4 167.4 %copy-start.62 = (f32[768]{0:T(1024)S(1)}, f32[768]{0:T(1024)}, u32[]{:S(2)}) copy-start(f32[768]{0:T(1024)} %convert_element_type.494) | copy-start | bytes 9220 | tf_op jit(solution)/shard_map/while
  921.4 56.0 %all-gather.39.cloned.1.call-start = ((), (), s32[]{:S(2)}) async-start(), calls=%async_computation.25 | async-start | bytes 1216512 | tf_op jit(solution)/shard_map/while/body/eval_jaxpr/all_gather | solution.py:43
  921.9 111.0 %all-gather.33.cloned.1.call-start = ((), (), s32[]{:S(2)}) async-start(), calls=%async_computation.22 | async-start | bytes 1216512 | tf_op jit(solution)/shard_map/while/body/eval_jaxpr/all_gather | solution.py:42
  922.5 166.2 %all-gather.37.cloned.1.call-start = ((), (), s32[]{:S(2)}) async-start(), calls=%async_computation.24 | async-start | bytes 1216512 | tf_op jit(solution)/shard_map/while/body/eval_jaxpr/all_gather | solution.py:40
  923.3 202.8 %all-gather.41.cloned.1.call-start = ((), (), s32[]{:S(2)}) async-start(), calls=%async_computation.26 | async-start | bytes 1966080 | tf_op jit(solution)/shard_map/while/body/eval_jaxpr/all_gather | solution.py:90
  980.0 183.5 %all-gather.35.cloned.1.call-start = ((), (), s32[]{:S(2)}) async-start(), calls=%async_computation.23 | async-start | bytes 1966080 | tf_op jit(solution)/shard_map/while/body/eval_jaxpr/all_gather | solution.py:89
  1035.6 183.7 %all-gather.43.cloned.1.call-start = ((), (), s32[]{:S(2)}) async-start(), calls=%async_computation.27 | async-start | bytes 1216512 | tf_op jit(solution)/shard_map/while/body/eval_jaxpr/all_gather | solution.py:45
  1036.3 248.3 %all-gather.45.cloned.1.call-start = ((), (), s32[]{:S(2)}) async-start(), calls=%async_computation.28 | async-start | bytes 4866048 | tf_op jit(solution)/shard_map/while/body/eval_jaxpr/all_gather | solution.py:49
  1037.0 312.2 %all-gather.47.cloned.1.call-start = ((), (), s32[]{:S(2)}) async-start(), calls=%async_computation.29 | async-start | bytes 4866048 | tf_op jit(solution)/shard_map/while/body/eval_jaxpr/all_gather | solution.py:51
  1037.6 391.2 %reduce-scatter.21.cloned.1.call-start = ((), (), s32[]{:S(2)}) async-start(), calls=%async_computation.30 | async-start | bytes 1966080 | tf_op jit(solution)/shard_map/while/body/eval_jaxpr/reduce_scatter | solution.py:214
  1389.1 70.4 %reduce-scatter.23.cloned.1.call-start = ((), (), s32[]{:S(2)}) async-start(), calls=%async_computation.31 | async-start | bytes 1966080 | tf_op jit(solution)/shard_map/while/body/eval_jaxpr/reduce_scatter | solution.py:220
  1467.5 56.4 %all-gather.39.cloned.1.call-start = ((), (), s32[]{:S(2)}) async-start(), calls=%async_computation.25 | async-start | bytes 1216512 | tf_op jit(solution)/shard_map/while/body/eval_jaxpr/all_gather | solution.py:43
  1468.1 111.6 %all-gather.33.cloned.1.call-start = ((), (), s32[]{:S(2)}) async-start(), calls=%async_computation.22 | async-start | bytes 1216512 | tf_op jit(solution)/shard_map/while/body/eval_jaxpr/all_gather | solution.py:42
  1468.8 166.6 %all-gather.37.cloned.1.call-start = ((), (), s32[]{:S(2)}) async-start(), calls=%async_computation.24 | async-start | bytes 1216512 | tf_op jit(solution)/shard_map/while/body/eval_jaxpr/all_gather | solution.py:40
  1469.6 203.2 %all-gather.41.cloned.1.call-start = ((), (), s32[]{:S(2)}) async-start(), calls=%async_computation.26 | async-start | bytes 1966080 | tf_op jit(solution)/shard_map/while/body/eval_jaxpr/all_gather | solution.py:90
  1526.6 183.7 %all-gather.35.cloned.1.call-start = ((), (), s32[]{:S(2)}) async-start(), calls=%async_computation.23 | async-start | bytes 1966080 | tf_op jit(solution)/shard_map/while/body/eval_jaxpr/all_gather | solution.py:89
  1582.3 183.7 %all-gather.43.cloned.1.call-start = ((), (), s32[]{:S(2)}) async-start(), calls=%async_computation.27 | async-start | bytes 1216512 | tf_op jit(solution)/shard_map/while/body/eval_jaxpr/all_gather | solution.py:45
  1583.0 248.2 %all-gather.45.cloned.1.call-start = ((), (), s32[]{:S(2)}) async-start(), calls=%async_computation.28 | async-start | bytes 4866048 | tf_op jit(solution)/shard_map/while/body/eval_jaxpr/all_gather | solution.py:49
  1583.6 312.3 %all-gather.47.cloned.1.call-start = ((), (), s32[]{:S(2)}) async-start(), calls=%async_computation.29 | async-start | bytes 4866048 | tf_op jit(solution)/shard_map/while/body/eval_jaxpr/all_gather | solution.py:51
  1584.3 398.7 %reduce-scatter.21.cloned.1.call-start = ((), (), s32[]{:S(2)}) async-start(), calls=%async_computation.30 | async-start | bytes 1966080 | tf_op jit(solution)/shard_map/while/body/eval_jaxpr/reduce_scatter | solution.py:214
  1935.8 70.4 %reduce-scatter.23.cloned.1.call-start = ((), (), s32[]{:S(2)}) async-start(), calls=%async_computation.31 | async-start | bytes 1966080 | tf_op jit(solution)/shard_map/while/body/eval_jaxpr/reduce_scatter | solution.py:220
  2014.2 104.9 %reduce-scatter.9.cloned.1.call-start = ((), (), s32[]{:S(2)}) async-start(), calls=%async_computation.8 | async-start | bytes 2433024 | tf_op jit(solution)/shard_map/reduce_scatter | solution.py:324
  2014.8 208.7 %reduce-scatter.11.cloned.1.call-start = ((), (), s32[]{:S(2)}) async-start(), calls=%async_computation.9 | async-start | bytes 2433024 | tf_op jit(solution)/shard_map/reduce_scatter | solution.py:324
  2015.4 312.4 %reduce-scatter.13.cloned.1.call-start = ((), (), s32[]{:S(2)}) async-start(), calls=%async_computation.10 | async-start | bytes 2433024 | tf_op jit(solution)/shard_map/reduce_scatter | solution.py:324
  2015.9 416.3 %reduce-scatter.15.cloned.1.call-start = ((), (), s32[]{:S(2)}) async-start(), calls=%async_computation.11 | async-start | bytes 2433024 | tf_op jit(solution)/shard_map/reduce_scatter | solution.py:324
  2016.7 557.3 %reduce-scatter.17.cloned.1.call-start = ((), (), s32[]{:S(2)}) async-start(), calls=%async_computation.12 | async-start | bytes 9732096 | tf_op jit(solution)/shard_map/reduce_scatter | solution.py:324
  2017.4 698.3 %reduce-scatter.19.cloned.1.call-start = ((), (), s32[]{:S(2)}) async-start(), calls=%async_computation.13 | async-start | bytes 9732096 | tf_op jit(solution)/shard_map/reduce_scatter | solution.py:324
  (126 other events, 2823.6 us)
Sparse Core Ops, SparseCore 0:
  11.9 56.9 all-gather.22
  71.7 52.8 all-gather.16
  127.4 52.9 all-gather.20
  182.3 35.9 all-gather.24
  220.3 35.8 all-gather.18
  258.9 52.8 all-gather.26
  314.6 62.5 all-gather.28
  379.9 61.8 all-gather.30
  458.4 52.5 all-gather.22
  513.6 52.9 all-gather.16
  569.4 52.9 all-gather.20
  624.4 35.9 all-gather.24
  662.5 35.8 all-gather.18
  701.1 52.8 all-gather.26
  756.6 62.5 all-gather.28
  821.8 61.8 all-gather.30
  924.7 52.6 all-gather.38
  980.0 52.9 all-gather.32
  1035.7 52.8 all-gather.36
  1090.1 35.9 all-gather.40
  1127.7 35.8 all-gather.34
  1166.4 52.8 all-gather.42
  1222.1 62.5 all-gather.44
  1287.3 61.8 all-gather.46
  1389.2 33.7 reduce-scatter.20
  1425.2 34.3 reduce-scatter.22
  1470.8 53.0 all-gather.38
  1526.7 52.8 all-gather.32
  1582.5 52.9 all-gather.36
  1636.8 35.9 all-gather.40
  1674.4 35.8 all-gather.34
  1713.1 52.8 all-gather.42
  1768.7 62.5 all-gather.44
  1834.0 61.8 all-gather.46
  1935.9 33.7 reduce-scatter.20
  1971.9 34.3 reduce-scatter.22
Sparse Core Ops, SparseCore 1:
  2020.5 98.5 reduce-scatter.8
  2124.8 98.6 reduce-scatter.10
  2229.2 98.5 reduce-scatter.12
  2333.7 98.5 reduce-scatter.14
  2438.8 135.2 reduce-scatter.16
  2580.5 135.2 reduce-scatter.18
where the time goes:
time: 2740 us; the launch traced here: 2720 us
  waiting for transfers between devices  2090 us (76%)
  matrix products  274 us (10%)
  blocking collectives  201 us (7%)
  local copies, waits for them, and re-layouts  77.8 us (3%)
  other arithmetic  38.4 us (1%)
    reduce_scatter x6, waiting for transfers between devices, per_device(): lax.psum_scatter(totals, ('dp', 'ctx'), scatter_dimension=0, tiled=True)  652 us
    all_gather x4, waiting for transfers between devices, fetch(): lax.all_gather(shards[11], ('dp', 'ctx'), axis=0, tiled=True)  256 us
    all_gather x4, waiting for transfers between devices, fetch(): lax.all_gather(shards[13], ('dp', 'ctx'), axis=0, tiled=True)  245 us
    all_gather x4, waiting for transfers between devices, fetch(): lax.all_gather(shards[2], ('dp', 'ctx'), axis=0, tiled=True)  195 us
    while x4, blocking collectives  161 us
    all_gather x4, waiting for transfers between devices, fetch(): lax.all_gather(shards[7], ('dp', 'ctx'), axis=0, tiled=True)  155 us
    all_gather x4, waiting for transfers between devices, forward(): lax.all_gather(value_rows, 'ctx', axis=0, tiled=True)  143 us
    all_gather x4, waiting for transfers between devices, forward(): lax.all_gather(key_rows, 'ctx', axis=0, tiled=True)  142 us
  transfers between devices with their start and end apart: 42, of which 40 were waited for; matrix products, arithmetic and copies ran while one was open for 10% of the time, Pallas kernels for 0%

commit v1 on v0

--- a/solution.py
+++ b/solution.py
@@ -5,6 +5,18 @@
 
 H = 12
 HD = 64
+
+
+def gather_around(shard, axis, dim):
+    ways, here, step = (lax.axis_size(axis), lax.axis_index(axis), shard.shape[dim])
+    shape = [n * ways if d == dim else n for d, n in enumerate(shard.shape)]
+    full = lax.dynamic_update_slice_in_dim(
+        jnp.zeros(shape, shard.dtype), shard, here * step, axis=dim
+    )
+    for far in range(1, ways):
+        shard = lax.ppermute(shard, axis, [(d, (d + 1) % ways) for d in range(ways)])
+        full = lax.dynamic_update_slice_in_dim(full, shard, (here - far) % ways * step, axis=dim)
+    return full
 
 
 def layer_norm(tok_rows, gain, shift):
@@ -87,7 +99,7 @@
     ).astype(jnp.bfloat16)
     all_keys, all_values = (
         lax.all_gather(key_rows, "ctx", axis=0, tiled=True),
-        lax.all_gather(value_rows, "ctx", axis=0, tiled=True),
+        gather_around(value_rows, "ctx", 0),
     )
     total_rows = all_keys.shape[0]
     query_heads = queries.reshape(seq_rows, H, HD)

time: 2740 us -> 2600 us (0.949)
  waiting for transfers between devices: 2090 us -> 1940 us
    all_gather x4 -> x0, waiting for transfers between devices: 143 us -> none  [forward(): lax.all_gather(value_rows, 'ctx', axis=0, tiled=True)]
    all_gather x4, waiting for transfers between devices: 116 us -> 21.4 us  [fetch(): lax.all_gather(shards[4], ('dp', 'ctx'), axis=0, tiled=True)]
    all_gather x4, waiting for transfers between devices: 117 us -> 204 us  [fetch(): lax.all_gather(shards[5], ('dp', 'ctx'), axis=0, tiled=True)]
    ppermute x0 -> x12, waiting for transfers between devices: none -> 86.8 us  [gather_around(): lax.ppermute(shard, axis, [(d, (d + 1) % ways) for d in range(ways)])]
    all_gather x4, waiting for transfers between devices: 195 us -> 123 us  [fetch(): lax.all_gather(shards[2], ('dp', 'ctx'), axis=0, tiled=True)]
  transfers between devices with their start and end apart: 42 -> 50, of which waited for: 40 -> 44; matrix products, arithmetic and copies ran while one was open for 10% -> 10% of each run, Pallas kernels for 0% -> 0%
where the time goes in v1:
time: 2600 us; the launch traced here: 2580 us
  waiting for transfers between devices  1940 us (75%)
  matrix products  269 us (10%)
  blocking collectives  201 us (8%)
  local copies, waits for them, and re-layouts  85.9 us (3%)
  other arithmetic  41.9 us (2%)
  loops' own time  27.8 us (1%)
    reduce_scatter x6, waiting for transfers between devices, per_device(): lax.psum_scatter(totals, ('dp', 'ctx'), scatter_dimension=0, tiled=True)  652 us
    all_gather x4, waiting for transfers between devices, fetch(): lax.all_gather(shards[11], ('dp', 'ctx'), axis=0, tiled=True)  256 us
    all_gather x4, waiting for transfers between devices, fetch(): lax.all_gather(shards[13], ('dp', 'ctx'), axis=0, tiled=True)  245 us
    all_gather x4, waiting for transfers between devices, fetch(): lax.all_gather(shards[5], ('dp', 'ctx'), axis=0, tiled=True)  204 us
    while x4, blocking collectives  161 us
    all_gather x4, waiting for transfers between devices, fetch(): lax.all_gather(shards[7], ('dp', 'ctx'), axis=0, tiled=True)  158 us
    all_gather x4, waiting for transfers between devices, forward(): lax.all_gather(key_rows, 'ctx', axis=0, tiled=True)  125 us
    all_gather x4, waiting for transfers between devices, fetch(): lax.all_gather(shards[2], ('dp', 'ctx'), axis=0, tiled=True)  123 us
  transfers between devices with their start and end apart: 50, of which 44 were waited for; matrix products, arithmetic and copies ran while one was open for 10% of the time, Pallas kernels for 0%

profile of v1, /device:TPU:0, one launch (start us, length us, event | category | flops | bytes accessed | tf_op | source)
XLA Modules:
  0.0 2585.0 jit_solution(11883410308774798047)
XLA Ops:
  9.1 820.5 %while.55 = (s32[]{:T(128)}, bf16[2,256,768]{2,1,0:T(8,128)(2,1)}, bf16[2,256,768]{2,1,0:T(8,128)(2,1)}, bf16[24]{0:T(256)(128)(2,1)}, bf16[24]{0:T(256)(128)(2,...) while((s32[]{:T(128)}, bf16[2,256,768]{2,1,0:T(8,128)(2,1)}, ...), condition=%wide.region_7.8_spmd, body=%wide.region_0.7_spmd.sunk | while | flops 4508832256 | bytes 134492976 | solution.py:319
  18.9 42.5 %all-reduce.39 = (bf16[768]{0:T(1024)(128)(2,1)S(1)}, bf16[768]{0:T(1024)(128)(2,1)S(1)}, bf16[768]{0:T(1024)(128)(2,1)S(1)}, bf16[768]{0:T(1024)(128)(2,1)S(1)}...) all-reduce(bf16[768]{0:T(1024)(128)(2,1)S(1)} %dynamic-update-slice, ...), channel_id=1, replica_groups=mesh['dp'=8,'ctx'=4] {'dp','ctx'}, use_global_device_ids=true, to_apply=%add.2 | all-reduce | flops 9216 | bytes 36864 | tf_op jit(solution)/shard_map/while
  74.4 51.0 %all-gather.15.cloned.1.call-done = bf16[768,768]{1,0:T(8,128)(2,1)} async-done(((bf16[24,768]{1,0:T(8,128)(2,1)}), bf16[768,768]{1,0:T(8,128)(2,1)}) %all-gather.15.cloned.1.call-update) | async-done | bytes 1179664 | tf_op jit(solution)/shard_map/while/body/eval_jaxpr/all_gather | solution.py:55
  127.9 12.7 collective-permute-done
  152.9 34.1 %all-gather.17.cloned.1.call-done = bf16[768,768]{1,0:T(8,128)(2,1)} async-done(((bf16[24,768]{1,0:T(8,128)(2,1)}), bf16[768,768]{1,0:T(8,128)(2,1)}) %all-gather.17.cloned.1.call-update) | async-done | bytes 1179664 | tf_op jit(solution)/shard_map/while/body/eval_jaxpr/all_gather | solution.py:52
  193.1 31.3 %all-gather.21.cloned.1.call-done = bf16[1024,768]{1,0:T(8,128)(2,1)} async-done(((bf16[256,768]{1,0:T(8,128)(2,1)}), bf16[1024,768]{1,0:T(8,128)(2,1)}) %all-gather.21.cloned.1.call-update) | async-done | bytes 1572880 | tf_op jit(solution)/shard_map/while/body/eval_jaxpr/all_gather | solution.py:101
  240.5 39.5 %all-gather.23.cloned.1.call-done = bf16[768,768]{1,0:T(8,128)(2,1)} async-done(((bf16[24,768]{1,0:T(8,128)(2,1)}), bf16[768,768]{1,0:T(8,128)(2,1)}) %all-gather.23.cloned.1.call-update) | async-done | bytes 1179664 | tf_op jit(solution)/shard_map/while/body/eval_jaxpr/all_gather | solution.py:57
  282.1 63.1 %all-gather.25.cloned.1.call-done = bf16[3072,768]{1,0:T(8,128)(2,1)} async-done(((bf16[96,768]{1,0:T(8,128)(2,1)}), bf16[3072,768]{1,0:T(8,128)(2,1)}) %all-gather.25.cloned.1.call-update) | async-done | bytes 4718608 | tf_op jit(solution)/shard_map/while/body/eval_jaxpr/all_gather | solution.py:63
  345.2 64.7 %all-gather.27.cloned.1.call-done = bf16[768,3072]{1,0:T(8,128)(2,1)} async-done(((bf16[24,3072]{1,0:T(8,128)(2,1)}), bf16[768,3072]{1,0:T(8,128)(2,1)}) %all-gather.27.cloned.1.call-update) | async-done | bytes 4718608 | tf_op jit(solution)/shard_map/while/body/eval_jaxpr/all_gather | solution.py:61
  409.9 12.9 fusion.316
  433.4 39.8 %all-reduce.39 = (bf16[768]{0:T(1024)(128)(2,1)S(1)}, bf16[768]{0:T(1024)(128)(2,1)S(1)}, bf16[768]{0:T(1024)(128)(2,1)S(1)}, bf16[768]{0:T(1024)(128)(2,1)S(1)}...) all-reduce(bf16[768]{0:T(1024)(128)(2,1)S(1)} %dynamic-update-slice, ...), channel_id=1, replica_groups=mesh['dp'=8,'ctx'=4] {'dp','ctx'}, use_global_device_ids=true, to_apply=%add.2 | all-reduce | flops 9216 | bytes 36864 | tf_op jit(solution)/shard_map/while
  484.6 51.1 %all-gather.15.cloned.1.call-done = bf16[768,768]{1,0:T(8,128)(2,1)} async-done(((bf16[24,768]{1,0:T(8,128)(2,1)}), bf16[768,768]{1,0:T(8,128)(2,1)}) %all-gather.15.cloned.1.call-update) | async-done | bytes 1179664 | tf_op jit(solution)/shard_map/while/body/eval_jaxpr/all_gather | solution.py:55
  538.2 12.7 collective-permute-done
  563.2 29.6 %all-gather.17.cloned.1.call-done = bf16[768,768]{1,0:T(8,128)(2,1)} async-done(((bf16[24,768]{1,0:T(8,128)(2,1)}), bf16[768,768]{1,0:T(8,128)(2,1)}) %all-gather.17.cloned.1.call-update) | async-done | bytes 1179664 | tf_op jit(solution)/shard_map/while/body/eval_jaxpr/all_gather | solution.py:52
  598.9 31.4 %all-gather.21.cloned.1.call-done = bf16[1024,768]{1,0:T(8,128)(2,1)} async-done(((bf16[256,768]{1,0:T(8,128)(2,1)}), bf16[1024,768]{1,0:T(8,128)(2,1)}) %all-gather.21.cloned.1.call-update) | async-done | bytes 1572880 | tf_op jit(solution)/shard_map/while/body/eval_jaxpr/all_gather | solution.py:101
  646.4 39.5 %all-gather.23.cloned.1.call-done = bf16[768,768]{1,0:T(8,128)(2,1)} async-done(((bf16[24,768]{1,0:T(8,128)(2,1)}), bf16[768,768]{1,0:T(8,128)(2,1)}) %all-gather.23.cloned.1.call-update) | async-done | bytes 1179664 | tf_op jit(solution)/shard_map/while/body/eval_jaxpr/all_gather | solution.py:57
  688.0 63.2 %all-gather.25.cloned.1.call-done = bf16[3072,768]{1,0:T(8,128)(2,1)} async-done(((bf16[96,768]{1,0:T(8,128)(2,1)}), bf16[3072,768]{1,0:T(8,128)(2,1)}) %all-gather.25.cloned.1.call-update) | async-done | bytes 4718608 | tf_op jit(solution)/shard_map/while/body/eval_jaxpr/all_gather | solution.py:63
  751.2 64.6 %all-gather.27.cloned.1.call-done = bf16[768,3072]{1,0:T(8,128)(2,1)} async-done(((bf16[24,3072]{1,0:T(8,128)(2,1)}), bf16[768,3072]{1,0:T(8,128)(2,1)}) %all-gather.27.cloned.1.call-update) | async-done | bytes 4718608 | tf_op jit(solution)/shard_map/while/body/eval_jaxpr/all_gather | solution.py:61
  815.8 12.9 fusion.316
  830.5 1045.5 %while.56 = (s32[]{:T(128)}, f32[768]{0:T(1024)}, f32[768]{0:T(1024)}, f32[768,768]{1,0:T(8,128)}, f32[768]{0:T(1024)}, /*index=5*/f32[768,768]{1,0:T(8,128)}, f...) while((s32[]{:T(128)}, f32[768]{0:T(1024)}, ...), condition=%wide.region_31.32_spmd.clone, body=%wide.region_8.31_spmd.clone.sunk | while | flops 12278196224 | bytes 527633952 | solution.py:335
  862.0 39.6 %all-reduce.40 = (bf16[768]{0:T(1024)(128)(2,1)S(1)}, bf16[768]{0:T(1024)(128)(2,1)S(1)}, bf16[3072]{0:T(1024)(128)(2,1)S(1)}, bf16[768]{0:T(1024)(128)(2,1)S(1)...) all-reduce(bf16[768]{0:T(1024)(128)(2,1)S(1)} %dynamic-update-slice, ...), channel_id=1, replica_groups=mesh['dp'=8,'ctx'=4] {'dp','ctx'}, use_global_device_ids=true, to_apply=%add.10 | all-reduce | flops 8448 | bytes 33792 | tf_op jit(solution)/shard_map/while
  914.3 50.7 %all-gather.35.cloned.1.call-done = bf16[768,768]{1,0:T(8,128)(2,1)} async-done(((bf16[24,768]{1,0:T(8,128)(2,1)}), bf16[768,768]{1,0:T(8,128)(2,1)}) %all-gather.35.cloned.1.call-update) | async-done | bytes 1179664 | tf_op jit(solution)/shard_map/while/body/eval_jaxpr/all_gather | solution.py:55
  967.5 12.7 collective-permute-done.3
  992.5 29.6 %all-gather.33.cloned.1.call-done = bf16[768,768]{1,0:T(8,128)(2,1)} async-done(((bf16[24,768]{1,0:T(8,128)(2,1)}), bf16[768,768]{1,0:T(8,128)(2,1)}) %all-gather.33.cloned.1.call-update) | async-done | bytes 1179664 | tf_op jit(solution)/shard_map/while/body/eval_jaxpr/all_gather | solution.py:52
  1028.4 31.1 %all-gather.31.cloned.1.call-done = bf16[1024,768]{1,0:T(8,128)(2,1)} async-done(((bf16[256,768]{1,0:T(8,128)(2,1)}), bf16[1024,768]{1,0:T(8,128)(2,1)}) %all-gather.31.cloned.1.call-update) | async-done | bytes 1572880 | tf_op jit(solution)/shard_map/while/body/eval_jaxpr/all_gather | solution.py:101
  1075.6 39.7 %all-gather.37.cloned.1.call-done = bf16[768,768]{1,0:T(8,128)(2,1)} async-done(((bf16[24,768]{1,0:T(8,128)(2,1)}), bf16[768,768]{1,0:T(8,128)(2,1)}) %all-gather.37.cloned.1.call-update) | async-done | bytes 1179664 | tf_op jit(solution)/shard_map/while/body/eval_jaxpr/all_gather | solution.py:57
  1117.4 63.1 %all-gather.39.cloned.1.call-done = bf16[768,3072]{1,0:T(8,128)(2,1)} async-done(((bf16[24,3072]{1,0:T(8,128)(2,1)}), bf16[768,3072]{1,0:T(8,128)(2,1)}) %all-gather.39.cloned.1.call-update) | async-done | bytes 4718608 | tf_op jit(solution)/shard_map/while/body/eval_jaxpr/all_gather | solution.py:61
  1186.0 59.2 %all-gather.41.cloned.1.call-done = bf16[3072,768]{1,0:T(8,128)(2,1)} async-done(((bf16[96,768]{1,0:T(8,128)(2,1)}), bf16[3072,768]{1,0:T(8,128)(2,1)}) %all-gather.41.cloned.1.call-update) | async-done | bytes 4718608 | tf_op jit(solution)/shard_map/while/body/eval_jaxpr/all_gather | solution.py:63
  1245.2 11.1 convert_reduce_fusion.15
  1326.8 28.8 %reduce-scatter.23.cloned.1.call-done = bf16[256,768]{0,1:T(8,128)(2,1)} async-done(((bf16[1024,768]{0,1:T(8,128)(2,1)}), bf16[256,768]{0,1:T(8,128)(2,1)}) %reduce-scatter.23.cloned.1.call-update) | async-done | bytes 393232 | tf_op jit(solution)/shard_map/while/body/eval_jaxpr/reduce_scatter | solution.py:232
  1372.1 39.6 %all-reduce.40 = (bf16[768]{0:T(1024)(128)(2,1)S(1)}, bf16[768]{0:T(1024)(128)(2,1)S(1)}, bf16[3072]{0:T(1024)(128)(2,1)S(1)}, bf16[768]{0:T(1024)(128)(2,1)S(1)...) all-reduce(bf16[768]{0:T(1024)(128)(2,1)S(1)} %dynamic-update-slice, ...), channel_id=1, replica_groups=mesh['dp'=8,'ctx'=4] {'dp','ctx'}, use_global_device_ids=true, to_apply=%add.10 | all-reduce | flops 8448 | bytes 33792 | tf_op jit(solution)/shard_map/while
  1424.8 50.8 %all-gather.35.cloned.1.call-done = bf16[768,768]{1,0:T(8,128)(2,1)} async-done(((bf16[24,768]{1,0:T(8,128)(2,1)}), bf16[768,768]{1,0:T(8,128)(2,1)}) %all-gather.35.cloned.1.call-update) | async-done | bytes 1179664 | tf_op jit(solution)/shard_map/while/body/eval_jaxpr/all_gather | solution.py:55
  1478.0 12.7 collective-permute-done.3
  1503.0 29.6 %all-gather.33.cloned.1.call-done = bf16[768,768]{1,0:T(8,128)(2,1)} async-done(((bf16[24,768]{1,0:T(8,128)(2,1)}), bf16[768,768]{1,0:T(8,128)(2,1)}) %all-gather.33.cloned.1.call-update) | async-done | bytes 1179664 | tf_op jit(solution)/shard_map/while/body/eval_jaxpr/all_gather | solution.py:52
  1538.9 31.1 %all-gather.31.cloned.1.call-done = bf16[1024,768]{1,0:T(8,128)(2,1)} async-done(((bf16[256,768]{1,0:T(8,128)(2,1)}), bf16[1024,768]{1,0:T(8,128)(2,1)}) %all-gather.31.cloned.1.call-update) | async-done | bytes 1572880 | tf_op jit(solution)/shard_map/while/body/eval_jaxpr/all_gather | solution.py:101
  1586.1 39.7 %all-gather.37.cloned.1.call-done = bf16[768,768]{1,0:T(8,128)(2,1)} async-done(((bf16[24,768]{1,0:T(8,128)(2,1)}), bf16[768,768]{1,0:T(8,128)(2,1)}) %all-gather.37.cloned.1.call-update) | async-done | bytes 1179664 | tf_op jit(solution)/shard_map/while/body/eval_jaxpr/all_gather | solution.py:57
  1627.9 63.2 %all-gather.39.cloned.1.call-done = bf16[768,3072]{1,0:T(8,128)(2,1)} async-done(((bf16[24,3072]{1,0:T(8,128)(2,1)}), bf16[768,3072]{1,0:T(8,128)(2,1)}) %all-gather.39.cloned.1.call-update) | async-done | bytes 4718608 | tf_op jit(solution)/shard_map/while/body/eval_jaxpr/all_gather | solution.py:61
  1696.6 59.0 %all-gather.41.cloned.1.call-done = bf16[3072,768]{1,0:T(8,128)(2,1)} async-done(((bf16[96,768]{1,0:T(8,128)(2,1)}), bf16[3072,768]{1,0:T(8,128)(2,1)}) %all-gather.41.cloned.1.call-update) | async-done | bytes 4718608 | tf_op jit(solution)/shard_map/while/body/eval_jaxpr/all_gather | solution.py:63
  1755.7 11.1 convert_reduce_fusion.15
  1830.5 12.2 select_add_fusion.38
  1844.6 21.3 reduce-scatter.23.cloned.1.call-done
  1880.1 40.0 %all-reduce.36 = (f32[768]{0:T(1024)S(1)}, f32[768]{0:T(1024)S(1)}, f32[768]{0:T(1024)S(1)}, f32[768]{0:T(1024)S(1)}, f32[768]{0:T(1024)S(1)}, /*index=5*/f32[76...) all-reduce(f32[768]{0:T(1024)S(1)} %copy-done.64, ...), channel_id=4, replica_groups=mesh['dp'=8,'ctx'=4] {'dp','ctx'}, use_global_device_ids=true, to_apply=%region_32.33.clone | all-reduce | flops 9216 | bytes 73728
  1925.3 55.6 %reduce-scatter.9.cloned.1.call-done = f32[24,768]{1,0:T(8,128)} async-done(((f32[768,768]{1,0:T(8,128)}), f32[24,768]{1,0:T(8,128)}) %reduce-scatter.9.cloned.1.call-update) | async-done | bytes 73744 | tf_op jit(solution)/shard_map/reduce_scatter | solution.py:336
  1980.9 104.4 %reduce-scatter.11.cloned.1.call-done = f32[24,768]{1,0:T(8,128)} async-done(((f32[768,768]{1,0:T(8,128)}), f32[24,768]{1,0:T(8,128)}) %reduce-scatter.11.cloned.1.call-update) | async-done | bytes 73744 | tf_op jit(solution)/shard_map/reduce_scatter | solution.py:336
  2085.3 104.4 %reduce-scatter.13.cloned.1.call-done = f32[24,768]{1,0:T(8,128)} async-done(((f32[768,768]{1,0:T(8,128)}), f32[24,768]{1,0:T(8,128)}) %reduce-scatter.13.cloned.1.call-update) | async-done | bytes 73744 | tf_op jit(solution)/shard_map/reduce_scatter | solution.py:336
  2189.7 104.5 %reduce-scatter.15.cloned.1.call-done = f32[24,768]{1,0:T(8,128)} async-done(((f32[768,768]{1,0:T(8,128)}), f32[24,768]{1,0:T(8,128)}) %reduce-scatter.15.cloned.1.call-update) | async-done | bytes 73744 | tf_op jit(solution)/shard_map/reduce_scatter | solution.py:336
  2294.2 141.7 %reduce-scatter.17.cloned.1.call-done = f32[24,3072]{1,0:T(8,128)} async-done(((f32[768,3072]{1,0:T(8,128)}), f32[24,3072]{1,0:T(8,128)}) %reduce-scatter.17.cloned.1.call-update) | async-done | bytes 294928 | tf_op jit(solution)/shard_map/reduce_scatter | solution.py:336
  2435.9 141.7 %reduce-scatter.19.cloned.1.call-done = f32[96,768]{1,0:T(8,128)} async-done(((f32[3072,768]{1,0:T(8,128)}), f32[96,768]{1,0:T(8,128)}) %reduce-scatter.19.cloned.1.call-update) | async-done | bytes 294928 | tf_op jit(solution)/shard_map/reduce_scatter | solution.py:336
  (705 shorter events, 416.8 us)
Async XLA Ops:
  9.1 60.6 %all-gather.19.cloned.1.call-start = ((), (), s32[]{:S(2)}) async-start(), calls=%async_computation.16 | async-start | bytes 1216512 | tf_op jit(solution)/shard_map/while/body/eval_jaxpr/all_gather | solution.py:54
  9.8 115.6 %all-gather.15.cloned.1.call-start = ((), (), s32[]{:S(2)}) async-start(), calls=%async_computation.14 | async-start | bytes 1216512 | tf_op jit(solution)/shard_map/while/body/eval_jaxpr/all_gather | solution.py:55
  10.6 176.5 %all-gather.17.cloned.1.call-start = ((), (), s32[]{:S(2)}) async-start(), calls=%async_computation.15 | async-start | bytes 1216512 | tf_op jit(solution)/shard_map/while/body/eval_jaxpr/all_gather | solution.py:52
  11.3 213.1 %all-gather.21.cloned.1.call-start = ((), (), s32[]{:S(2)}) async-start(), calls=%async_computation.17 | async-start | bytes 1966080 | tf_op jit(solution)/shard_map/while/body/eval_jaxpr/all_gather | solution.py:101
  72.5 207.5 %all-gather.23.cloned.1.call-start = ((), (), s32[]{:S(2)}) async-start(), calls=%async_computation.18 | async-start | bytes 1216512 | tf_op jit(solution)/shard_map/while/body/eval_jaxpr/all_gather | solution.py:57
  73.1 272.1 %all-gather.25.cloned.1.call-start = ((), (), s32[]{:S(2)}) async-start(), calls=%async_computation.19 | async-start | bytes 4866048 | tf_op jit(solution)/shard_map/while/body/eval_jaxpr/all_gather | solution.py:63
  73.6 336.3 %all-gather.27.cloned.1.call-start = ((), (), s32[]{:S(2)}) async-start(), calls=%async_computation.20 | async-start | bytes 4866048 | tf_op jit(solution)/shard_map/while/body/eval_jaxpr/all_gather | solution.py:61
  127.2 13.3 collective-permute-start
  140.5 12.3 collective-permute-start.1
  152.9 37.8 %collective-permute-start.2 = (bf16[256,768]{1,0:T(8,128)(2,1)S(1)}, bf16[256,768]{1,0:T(8,128)(2,1)}, u32[]{:S(2)}, u32[]{:S(2)}) collective-permute-start(bf16[256,768]{1,0:T(8,128)(2,1)S(1)} %collective-permute-done.1), channel_id=1, source_target_pairs={{0,1},{1,2},{2,3},{3,0},{4,5},{5,6},{6,7},{7,4},{8,9},{9,10},{10,1... | collective-permute-start | bytes 1179656 | tf_op jit(solution)/shard_map/while/body/eval_jaxpr/ppermute | solution.py:17
  423.7 56.2 %all-gather.19.cloned.1.call-start = ((), (), s32[]{:S(2)}) async-start(), calls=%async_computation.16 | async-start | bytes 1216512 | tf_op jit(solution)/shard_map/while/body/eval_jaxpr/all_gather | solution.py:54
  424.4 111.3 %all-gather.15.cloned.1.call-start = ((), (), s32[]{:S(2)}) async-start(), calls=%async_computation.14 | async-start | bytes 1216512 | tf_op jit(solution)/shard_map/while/body/eval_jaxpr/all_gather | solution.py:55
  425.2 167.6 %all-gather.17.cloned.1.call-start = ((), (), s32[]{:S(2)}) async-start(), calls=%async_computation.15 | async-start | bytes 1216512 | tf_op jit(solution)/shard_map/while/body/eval_jaxpr/all_gather | solution.py:52
  425.7 204.6 %all-gather.21.cloned.1.call-start = ((), (), s32[]{:S(2)}) async-start(), calls=%async_computation.17 | async-start | bytes 1966080 | tf_op jit(solution)/shard_map/while/body/eval_jaxpr/all_gather | solution.py:101
  482.7 203.2 %all-gather.23.cloned.1.call-start = ((), (), s32[]{:S(2)}) async-start(), calls=%async_computation.18 | async-start | bytes 1216512 | tf_op jit(solution)/shard_map/while/body/eval_jaxpr/all_gather | solution.py:57
  483.2 268.0 %all-gather.25.cloned.1.call-start = ((), (), s32[]{:S(2)}) async-start(), calls=%async_computation.19 | async-start | bytes 4866048 | tf_op jit(solution)/shard_map/while/body/eval_jaxpr/all_gather | solution.py:63
  484.0 331.8 %all-gather.27.cloned.1.call-start = ((), (), s32[]{:S(2)}) async-start(), calls=%async_computation.20 | async-start | bytes 4866048 | tf_op jit(solution)/shard_map/while/body/eval_jaxpr/all_gather | solution.py:61
  537.5 13.3 collective-permute-start
  550.8 12.3 collective-permute-start.1
  563.2 33.2 %collective-permute-start.2 = (bf16[256,768]{1,0:T(8,128)(2,1)S(1)}, bf16[256,768]{1,0:T(8,128)(2,1)}, u32[]{:S(2)}, u32[]{:S(2)}) collective-permute-start(bf16[256,768]{1,0:T(8,128)(2,1)S(1)} %collective-permute-done.1), channel_id=1, source_target_pairs={{0,1},{1,2},{2,3},{3,0},{4,5},{5,6},{6,7},{7,4},{8,9},{9,10},{10,1... | collective-permute-start | bytes 1179656 | tf_op jit(solution)/shard_map/while/body/eval_jaxpr/ppermute | solution.py:17
  853.4 56.0 %all-gather.29.cloned.1.call-start = ((), (), s32[]{:S(2)}) async-start(), calls=%async_computation.21 | async-start | bytes 1216512 | tf_op jit(solution)/shard_map/while/body/eval_jaxpr/all_gather | solution.py:54
  854.0 111.0 %all-gather.35.cloned.1.call-start = ((), (), s32[]{:S(2)}) async-start(), calls=%async_computation.24 | async-start | bytes 1216512 | tf_op jit(solution)/shard_map/while/body/eval_jaxpr/all_gather | solution.py:55
  854.6 167.5 %all-gather.33.cloned.1.call-start = ((), (), s32[]{:S(2)}) async-start(), calls=%async_computation.23 | async-start | bytes 1216512 | tf_op jit(solution)/shard_map/while/body/eval_jaxpr/all_gather | solution.py:52
  855.2 204.3 %all-gather.31.cloned.1.call-start = ((), (), s32[]{:S(2)}) async-start(), calls=%async_computation.22 | async-start | bytes 1966080 | tf_op jit(solution)/shard_map/while/body/eval_jaxpr/all_gather | solution.py:101
  912.2 203.1 %all-gather.37.cloned.1.call-start = ((), (), s32[]{:S(2)}) async-start(), calls=%async_computation.25 | async-start | bytes 1216512 | tf_op jit(solution)/shard_map/while/body/eval_jaxpr/all_gather | solution.py:57
  912.9 267.5 %all-gather.39.cloned.1.call-start = ((), (), s32[]{:S(2)}) async-start(), calls=%async_computation.26 | async-start | bytes 4866048 | tf_op jit(solution)/shard_map/while/body/eval_jaxpr/all_gather | solution.py:61
  913.5 331.7 %all-gather.41.cloned.1.call-start = ((), (), s32[]{:S(2)}) async-start(), calls=%async_computation.27 | async-start | bytes 4866048 | tf_op jit(solution)/shard_map/while/body/eval_jaxpr/all_gather | solution.py:63
  914.3 410.5 %reduce-scatter.21.cloned.1.call-start = ((), (), s32[]{:S(2)}) async-start(), calls=%async_computation.28 | async-start | bytes 1966080 | tf_op jit(solution)/shard_map/while/body/eval_jaxpr/reduce_scatter | solution.py:226
  966.9 13.3 collective-permute-start.3
  992.5 33.5 %collective-permute-start.5 = (bf16[256,768]{1,0:T(8,128)(2,1)S(1)}, bf16[256,768]{1,0:T(8,128)(2,1)}, u32[]{:S(2)}, u32[]{:S(2)}) collective-permute-start(bf16[256,768]{1,0:T(8,128)(2,1)S(1)} %collective-permute-done.4), channel_id=1, source_target_pairs={{0,1},{1,2},{2,3},{3,0},{4,5},{5,6},{6,7},{7,4},{8,9},{9,10},{10,1... | collective-permute-start | bytes 1179656 | tf_op jit(solution)/shard_map/while/body/eval_jaxpr/ppermute | solution.py:17
  1284.9 70.6 %reduce-scatter.23.cloned.1.call-start = ((), (), s32[]{:S(2)}) async-start(), calls=%async_computation.29 | async-start | bytes 1966080 | tf_op jit(solution)/shard_map/while/body/eval_jaxpr/reduce_scatter | solution.py:232
  1363.4 56.4 %all-gather.29.cloned.1.call-start = ((), (), s32[]{:S(2)}) async-start(), calls=%async_computation.21 | async-start | bytes 1216512 | tf_op jit(solution)/shard_map/while/body/eval_jaxpr/all_gather | solution.py:54
  1364.0 111.6 %all-gather.35.cloned.1.call-start = ((), (), s32[]{:S(2)}) async-start(), calls=%async_computation.24 | async-start | bytes 1216512 | tf_op jit(solution)/shard_map/while/body/eval_jaxpr/all_gather | solution.py:55
  1364.7 167.9 %all-gather.33.cloned.1.call-start = ((), (), s32[]{:S(2)}) async-start(), calls=%async_computation.23 | async-start | bytes 1216512 | tf_op jit(solution)/shard_map/while/body/eval_jaxpr/all_gather | solution.py:52
  1365.3 204.7 %all-gather.31.cloned.1.call-start = ((), (), s32[]{:S(2)}) async-start(), calls=%async_computation.22 | async-start | bytes 1966080 | tf_op jit(solution)/shard_map/while/body/eval_jaxpr/all_gather | solution.py:101
  1422.6 203.1 %all-gather.37.cloned.1.call-start = ((), (), s32[]{:S(2)}) async-start(), calls=%async_computation.25 | async-start | bytes 1216512 | tf_op jit(solution)/shard_map/while/body/eval_jaxpr/all_gather | solution.py:57
  1423.4 267.7 %all-gather.39.cloned.1.call-start = ((), (), s32[]{:S(2)}) async-start(), calls=%async_computation.26 | async-start | bytes 4866048 | tf_op jit(solution)/shard_map/while/body/eval_jaxpr/all_gather | solution.py:61
  1424.1 331.6 %all-gather.41.cloned.1.call-start = ((), (), s32[]{:S(2)}) async-start(), calls=%async_computation.27 | async-start | bytes 4866048 | tf_op jit(solution)/shard_map/while/body/eval_jaxpr/all_gather | solution.py:63
  1424.7 418.0 %reduce-scatter.21.cloned.1.call-start = ((), (), s32[]{:S(2)}) async-start(), calls=%async_computation.28 | async-start | bytes 1966080 | tf_op jit(solution)/shard_map/while/body/eval_jaxpr/reduce_scatter | solution.py:226
  1477.4 13.3 collective-permute-start.3
  1503.0 33.5 %collective-permute-start.5 = (bf16[256,768]{1,0:T(8,128)(2,1)S(1)}, bf16[256,768]{1,0:T(8,128)(2,1)}, u32[]{:S(2)}, u32[]{:S(2)}) collective-permute-start(bf16[256,768]{1,0:T(8,128)(2,1)S(1)} %collective-permute-done.4), channel_id=1, source_target_pairs={{0,1},{1,2},{2,3},{3,0},{4,5},{5,6},{6,7},{7,4},{8,9},{9,10},{10,1... | collective-permute-start | bytes 1179656 | tf_op jit(solution)/shard_map/while/body/eval_jaxpr/ppermute | solution.py:17
  1795.4 70.6 %reduce-scatter.23.cloned.1.call-start = ((), (), s32[]{:S(2)}) async-start(), calls=%async_computation.29 | async-start | bytes 1966080 | tf_op jit(solution)/shard_map/while/body/eval_jaxpr/reduce_scatter | solution.py:232
  1876.0 104.9 %reduce-scatter.9.cloned.1.call-start = ((), (), s32[]{:S(2)}) async-start(), calls=%async_computation.8 | async-start | bytes 2433024 | tf_op jit(solution)/shard_map/reduce_scatter | solution.py:336
  1876.6 208.7 %reduce-scatter.11.cloned.1.call-start = ((), (), s32[]{:S(2)}) async-start(), calls=%async_computation.9 | async-start | bytes 2433024 | tf_op jit(solution)/shard_map/reduce_scatter | solution.py:336
  1877.2 312.5 %reduce-scatter.13.cloned.1.call-start = ((), (), s32[]{:S(2)}) async-start(), calls=%async_computation.10 | async-start | bytes 2433024 | tf_op jit(solution)/shard_map/reduce_scatter | solution.py:336
  1877.8 416.5 %reduce-scatter.15.cloned.1.call-start = ((), (), s32[]{:S(2)}) async-start(), calls=%async_computation.11 | async-start | bytes 2433024 | tf_op jit(solution)/shard_map/reduce_scatter | solution.py:336
  1878.5 557.4 %reduce-scatter.17.cloned.1.call-start = ((), (), s32[]{:S(2)}) async-start(), calls=%async_computation.12 | async-start | bytes 9732096 | tf_op jit(solution)/shard_map/reduce_scatter | solution.py:336
  1879.2 698.4 %reduce-scatter.19.cloned.1.call-start = ((), (), s32[]{:S(2)}) async-start(), calls=%async_computation.13 | async-start | bytes 9732096 | tf_op jit(solution)/shard_map/reduce_scatter | solution.py:336
  (153 other events, 4863.2 us)
Sparse Core Ops, SparseCore 0:
  12.7 56.9 all-gather.18
  72.5 52.8 all-gather.14
  128.2 58.7 all-gather.16
  188.4 35.9 all-gather.20
  227.1 52.8 all-gather.22
  282.6 62.5 all-gather.24
  348.0 61.8 all-gather.26
  427.3 52.5 all-gather.18
  482.7 52.9 all-gather.14
  538.4 54.3 all-gather.16
  594.4 35.9 all-gather.20
  633.0 52.8 all-gather.22
  688.7 62.5 all-gather.24
  753.9 61.8 all-gather.26
  856.8 52.6 all-gather.28
  912.1 52.9 all-gather.34
  967.7 54.3 all-gather.32
  1023.5 35.9 all-gather.30
  1062.3 52.8 all-gather.36
  1117.9 62.5 all-gather.38
  1183.3 61.8 all-gather.40
  1285.0 33.7 reduce-scatter.20
  1321.1 34.3 reduce-scatter.22
  1366.7 53.0 all-gather.28
  1422.6 52.8 all-gather.34
  1478.2 54.3 all-gather.32
  1534.0 35.9 all-gather.30
  1572.8 52.8 all-gather.36
  1628.5 62.5 all-gather.38
  1693.7 61.8 all-gather.40
  1795.5 33.7 reduce-scatter.20
  1831.6 34.2 reduce-scatter.22
Sparse Core Ops, SparseCore 1:
  1882.3 98.5 reduce-scatter.8
  1986.7 98.6 reduce-scatter.10
  2091.0 98.6 reduce-scatter.12
  2195.6 98.6 reduce-scatter.14
  2300.7 135.1 reduce-scatter.16
  2442.4 135.2 reduce-scatter.18
